TPU v7x, 256 devices: a whole 4x4x8 slice. The times are simulated.
256 devices in a mesh: rep: 16 (over z_lo, x), shard: 16 (over z_hi, y, core).
Axes of the slice: x: 4, y: 4, z: 8 (z_hi: 2, z_lo: 4; z = z_hi * 4 + z_lo), core: 2. Of those that a mesh axis runs over, the one named last changes fastest.
Arguments:
- attn: bfloat16 [16, 6144, 2560], P('rep', 'shard'), may hold values from -6 to 6
- resid: bfloat16 [16, 6144, 2560], P('rep', 'shard'), may hold values from -200 to 200
- cotangent: bfloat16 [16, 6144, 2560], P('rep', 'shard'), may hold values from -6 to 6
- gain: float32 [2560], replicated, may hold values from 0.1 to 1.9
- numer: float32 [16, 2560, 2560], P('rep', 'shard'), may hold values from -6 to 6
- pweight: float32 [16], P('rep'), may hold values from 0.5 to 2
- round_bit: int32 [1], replicated, may hold values from 0 to 3
Outputs:
- new_numer: float32 [16, 2560, 2560], P('rep', 'shard')
- new_pweight: float32 [16], P('rep')
All inputs are finite; a program needn't handle non-finite values.
Results may differ from a plain program's by a relative error of at most 0.008.
Values may be sent and summed in bfloat16 or wider, within the bound.
No kernel may reach another device: no remote copies, remote signals or barrier semaphores. Data moves between devices by JAX's collectives and lax.ppermute only.
A program may use at most 192 MiB of HBM per device.

v0:
```python
import jax
import jax.numpy as jnp
from jax import lax
from jax.sharding import PartitionSpec as P

EPS = 1e-05
learning_rate = 0.5


def shortened(shard):

    def short(part):
        return part.astype(jnp.bfloat16) if part.dtype == jnp.float32 else part

    return jax.tree.map(short, shard)


def from_partner(shard, axis, apart):
    return lax.ppermute(shard, axis, [(i, i ^ 1 << apart) for i in range(lax.axis_size(axis))])


def on_device(attn, resid, cotangent, gain, numer, pweight, round_bit):
    acts = attn[0]
    weight_rows = (numer[0] / pweight[0]).astype(jnp.bfloat16)
    columns = acts
    pre = resid[0].astype(jnp.float32) + jnp.dot(
        columns,
        lax.all_gather(weight_rows, "shard", axis=0, tiled=True),
        preferred_element_type=jnp.float32,
    )
    inv = lax.rsqrt(jnp.mean(pre * pre, axis=1, keepdims=True) + EPS)
    normed = pre * inv
    dnorm = cotangent[0].astype(jnp.float32) * gain
    dpre = (inv * (dnorm - normed * jnp.mean(dnorm * normed, axis=1, keepdims=True))).astype(
        jnp.bfloat16
    )
    columns = acts
    grad = lax.psum_scatter(
        lax.dot_general(
            columns, dpre, (((0,), (0,)), ((), ())), preferred_element_type=jnp.float32
        ).astype(jnp.bfloat16),
        "shard",
        scatter_dimension=0,
        tiled=True,
    ).astype(jnp.float32)
    stepped = numer[0] - learning_rate * grad
    levels = lax.axis_size("rep").bit_length() - 1

    def pushed(bit):

        def send_pair(pair):
            return jax.tree.map(
                lambda part, own: part.astype(own.dtype),
                from_partner(shortened(pair), "rep", bit),
                pair,
            )

        return send_pair

    other_numer, other_weight = lax.switch(
        round_bit[0], [pushed(level) for level in range(levels)], (stepped, pweight)
    )
    new_numer = (0.5 * (stepped + other_numer))[None]
    new_pweight = 0.5 * (pweight + other_weight)
    return (new_numer, new_pweight)


def solution(mesh):
    in_specs = (
        P("rep", "shard", None),
        P("rep", "shard", None),
        P("rep", "shard", None),
        P(),
        P("rep", "shard", None),
        P("rep"),
        P(),
    )
    out_specs = (P("rep", "shard", None), P("rep"))
    return jax.shard_map(
        on_device, mesh=mesh, in_specs=in_specs, out_specs=out_specs, check_vma=False
    )
```

profile of v0, /device:TPU:32, one launch (start us, length us, event | category | flops | bytes accessed | tf_op | source)
XLA Modules:
  0.0 410.0 jit_solution(1422949947530526747)
XLA Ops:
  7.2 0.0 copy-start
  7.2 0.0 all-gather.2.cloned.1.call-start
  8.0 2.4 fusion.14
  10.4 0.0 all-gather.2.cloned.1.call-update
  10.5 0.0 reduce-scatter.4.cloned.1.call-start
  10.5 4.0 copy.18
  14.5 4.0 copy.19
  18.5 0.0 copy-start.4
  18.5 139.0 %all-gather.2.cloned.1.call-done = bf16[2560,2560]{1,0:T(8,128)(2,1)} async-done(((bf16[160,2560]{1,0:T(8,128)(2,1)}), bf16[2560,2560]{1,0:T(8,128)(2,1)}) %all-gather.2.cloned.1.call-update) | async-done | bytes 13107216 | tf_op jit(solution)/shard_map/all_gather | solution.py:28
  157.5 0.0 copy-done
  157.5 0.0 copy-start.2
  157.5 10.8 %multiply_reduce_fusion = (f32[384]{0:T(512)S(1)}, f32[384,2560]{0,1:T(8,128)S(1)}) fusion(bf16[2560,2560]{1,0:T(8,128)(2,1)} %all-gather.2.cloned.1.call-done, bf16[1,384,2560]{2,1,0:T(8,128)(2,1)S(1)} %copy-done, bf16[1,384,2560]{1,2,0:T(8,128)(2,1)} %copy.18), kind=kOutput, calls=%fused_computation.10 | convolution fusion | flops 5037096448 | bytes 20973056 | tf_op jit(solution)/shard_map/dot_general | solution.py:26
  168.3 0.0 copy-done.4
  168.3 0.0 copy-done.2
  168.3 0.7 fusion.4
  169.0 10.4 %fusion = bf16[2560,2560]{0,1:T(8,128)(2,1)} fusion(f32[384,2560]{0,1:T(8,128)S(1)} %get-tuple-element.59, bf16[1,384,2560]{1,2,0:T(8,128)(2,1)S(1)} %copy-done.2, bf16[1,384,2560]{2,1,0:T(8,128)(2,1)S(1)} %copy-done, f32[384]{0:T(512)S(1)} %broadcast_multiply_fusion, f32[2560]{0:T(1024)S(1)} %copy-done.4, f32[384]{0:T(512)S(1)} %add_rsqrt_fusion), kind=kOutput, calls=%fused_computation.1 | convolution fusion | flops 5046599680 | bytes 20984832 | tf_op jit(solution)/shard_map/dot_general | solution.py:39
  179.5 17.6 %copy.21 = bf16[2560,2560]{1,0:T(8,128)(2,1)} copy(bf16[2560,2560]{0,1:T(8,128)(2,1)} %fusion) | data formatting | bytes 26214400
  197.1 0.0 copy-start.3
  197.1 0.0 reduce-scatter.4.cloned.1.call-update
  197.9 175.3 %reduce-scatter.4.cloned.1.call-done = bf16[160,2560]{1,0:T(8,128)(2,1)} async-done(((bf16[2560,2560]{1,0:T(8,128)(2,1)}), bf16[160,2560]{1,0:T(8,128)(2,1)}) %reduce-scatter.4.cloned.1.call-update) | async-done | bytes 819216 | tf_op jit(solution)/shard_map/reduce_scatter | solution.py:38
  373.2 0.0 copy-done.3
  373.2 2.5 bitcast_subtract_fusion
  375.7 23.0 %conditional.4 = (f32[160,2560]{1,0:T(8,128)}, f32[1]{0:T(128)}) conditional(s32[]{:T(128)} %bitcast.7, (f32[160,2560]{1,0:T(8,128)}, f32[1]{0:T(128)}) %tuple.50, (f32[160,2560]{1,0:T(8,128)}, f32[1]{0:T(128)}) %tuple.50, (f32[160,2560]{1,0:T(8,128)}, f32[1]{0:T(128)}) %tuple.50, (f32[160,2560]{1,0:T(8,128)}, ...), branch_computations={%region_3.0_spmd, %region_4.0_spmd, %region_5.0_spmd, %region_6.0_... | conditional | flops 819202 | bytes 8192116
  375.7 1.5 convert_element_type.70
  377.2 1.6 collective-permute-start
  379.4 16.2 %collective-permute-start.1 = (bf16[1]{0:T(256)(128)(2,1)}, bf16[1]{0:T(256)(128)(2,1)}, u32[]{:S(2)}, u32[]{:S(2)}) collective-permute-start(bf16[1]{0:T(256)(128)(2,1)} %convert_element_type.72), channel_id=1, source_target_pairs={{0,16},{16,0},{32,48},{48,32},{64,80},{80,64},{96,112},{112,96},{1... | collective-permute-start | bytes 14 | tf_op jit(solution)/shard_map/cond/branch_0_fun/ppermute | solution.py:19
  395.6 1.1 collective-permute-done.1
  397.3 0.0 collective-permute-done
  397.3 1.4 convert_element_type.108
  398.7 0.0 copy-start.1
  398.7 3.4 multiply_bitcast_fusion
  402.1 0.0 copy-done.1
  (2 shorter events, 0.0 us)
Async XLA Ops:
  7.2 150.3 %copy-start = (bf16[1,384,2560]{2,1,0:T(8,128)(2,1)S(1)}, bf16[1,384,2560]{2,1,0:T(8,128)(2,1)}, u32[]{:S(2)}) copy-start(bf16[1,384,2560]{2,1,0:T(8,128)(2,1)} %param.11) | copy-start | bytes 5898244
  7.2 150.3 %all-gather.2.cloned.1.call-start = ((), (), s32[]{:S(2)}) async-start(), calls=%async_computation.1 | async-start | bytes 13926400 | tf_op jit(solution)/shard_map/all_gather | solution.py:28
  10.5 362.7 %reduce-scatter.4.cloned.1.call-start = ((), (), s32[]{:S(2)}) async-start(), calls=%async_computation.2 | async-start | bytes 13926400 | tf_op jit(solution)/shard_map/reduce_scatter | solution.py:38
  18.5 149.8 %copy-start.4 = (f32[2560]{0:T(1024)S(1)}, f32[2560]{0:T(1024)}, u32[]{:S(2)}) copy-start(f32[2560]{0:T(1024)} %param.14) | copy-start | bytes 30724
  157.5 10.8 %copy-start.2 = (bf16[1,384,2560]{1,2,0:T(8,128)(2,1)S(1)}, bf16[1,384,2560]{1,2,0:T(8,128)(2,1)}, u32[]{:S(2)}) copy-start(bf16[1,384,2560]{1,2,0:T(8,128)(2,1)} %copy.19) | copy-start | bytes 5898244
  197.1 176.1 %copy-start.3 = (f32[1,160,2560]{2,1,0:T(8,128)S(1)}, f32[1,160,2560]{2,1,0:T(8,128)}, u32[]{:S(2)}) copy-start(f32[1,160,2560]{2,1,0:T(8,128)} %param.15) | copy-start | bytes 4915204
  377.2 20.1 %collective-permute-start = (bf16[160,2560]{1,0:T(8,128)(2,1)S(1)}, bf16[160,2560]{1,0:T(8,128)(2,1)S(1)}, u32[]{:S(2)}, u32[]{:S(2)}) collective-permute-start(bf16[160,2560]{1,0:T(8,128)(2,1)S(1)} %convert_element_type.70), channel_id=1, source_target_pairs={{0,16},{16,0},{32,48},{48,32},{64,80},{80,64},{96,112},{112,96},{1... | collective-permute-start | bytes 2457608 | tf_op jit(solution)/shard_map/cond/branch_0_fun/ppermute | solution.py:19
  379.4 17.3 %collective-permute-start.1 = (bf16[1]{0:T(256)(128)(2,1)}, bf16[1]{0:T(256)(128)(2,1)}, u32[]{:S(2)}, u32[]{:S(2)}) collective-permute-start(bf16[1]{0:T(256)(128)(2,1)} %convert_element_type.72), channel_id=1, source_target_pairs={{0,16},{16,0},{32,48},{48,32},{64,80},{80,64},{96,112},{112,96},{1... | collective-permute-start | bytes 14 | tf_op jit(solution)/shard_map/cond/branch_0_fun/ppermute | solution.py:19
  398.7 3.4 copy-start.1
Sparse Core Ops, SparseCore 0:
  11.3 146.1 all-gather.1
  197.2 175.8 reduce-scatter.3
where the time goes:
time: 411 us; the launch traced here: 410 us
  waiting for transfers between devices  315 us (77%)
  local copies, waits for them, and re-layouts  25.7 us (6%)
  matrix products  21.2 us (5%)
  starting transfers between devices  17.8 us (4%)
  between operations  16.8 us (4%)
  other arithmetic  11.9 us (3%)
    reduce_scatter x1, waiting for transfers between devices, on_device(): lax.psum_scatter(lax.dot_general(columns, dpre, (((0,), (0,)), ((), ())),...  175 us
    all_gather x1, waiting for transfers between devices, on_device(): lax.all_gather(weight_rows, 'shard', axis=0, tiled=True)  139 us
    unnamed x13, local copies, waits for them, and re-layouts  25.7 us
    ppermute x2, starting transfers between devices, from_partner(): lax.ppermute(shard, axis, [(i, i ^ 1 << apart) for i in range(lax.axis_si...  17.8 us
    dot_general x1, matrix products, on_device(): jnp.dot(columns, lax.all_gather(weight_rows, 'shard', axis=0, tiled=True)...  10.8 us
    dot_general x1, matrix products, on_device(): lax.dot_general(columns, dpre, (((0,), (0,)), ((), ())), preferred_elemen...  10.4 us
  transfers between devices with their start and end apart: 4, of which 3 were waited for; matrix products, arithmetic and copies ran while one was open for 2% of the time, Pallas kernels for 0%

commit v1 on v0

--- a/solution.py
+++ b/solution.py
@@ -1,3 +1,4 @@
+import functools
 import jax
 import jax.numpy as jnp
 from jax import lax
@@ -5,6 +6,16 @@
 
 EPS = 1e-05
 learning_rate = 0.5
+
+
+def screen_guide(view, dev_axis):
+    extra = jnp.concatenate(
+        lax.all_to_all(jnp.stack(lax.axis_size(dev_axis) * [view], axis=0), dev_axis, 0, 0), axis=0
+    )
+    return extra
+
+
+task_unite = functools.partial(screen_guide, dev_axis="shard")
 
 
 def shortened(shard):
@@ -24,9 +35,7 @@
     weight_rows = (numer[0] / pweight[0]).astype(jnp.bfloat16)
     columns = acts
     pre = resid[0].astype(jnp.float32) + jnp.dot(
-        columns,
-        lax.all_gather(weight_rows, "shard", axis=0, tiled=True),
-        preferred_element_type=jnp.float32,
+        columns, task_unite(weight_rows), preferred_element_type=jnp.float32
     )
     inv = lax.rsqrt(jnp.mean(pre * pre, axis=1, keepdims=True) + EPS)
     normed = pre * inv

time: 411 us -> 666 us (1.62)
  waiting for transfers between devices: 315 us -> 545 us
  local copies, waits for them, and re-layouts: 25.7 us -> 43.1 us
  starting transfers between devices: 17.8 us -> 28.2 us
    all_to_all x0 -> x1, waiting for transfers between devices: none -> 326 us  [screen_guide(): lax.all_to_all(jnp.stack(lax.axis_size(dev_axis) * [view], axis=0), dev_a...]
    unnamed x2, waiting for transfers between devices: 0.03 us -> 218 us
    reduce_scatter x1 -> x0, waiting for transfers between devices: 175 us -> none  [on_device(): lax.psum_scatter(lax.dot_general(columns, dpre, (((0,), (0,)), ((), ())),...]
    all_gather x1 -> x0, waiting for transfers between devices: 139 us -> none  [on_device(): lax.all_gather(weight_rows, 'shard', axis=0, tiled=True)]
    all_to_all x0 -> x1, starting transfers between devices: none -> 10.3 us  [screen_guide(): lax.all_to_all(jnp.stack(lax.axis_size(dev_axis) * [view], axis=0), dev_a...]
    unnamed x13 -> x17, local copies, waits for them, and re-layouts: 25.7 us -> 35.1 us
    another operation x0 -> x2, local copies, waits for them, and re-layouts: none -> 7.93 us  [the longest x1 6.01 us: screen_guide(): jnp.stack(lax.axis_size(dev_axis) * [view], axis=0)]
where the time goes in v1:
time: 666 us; the launch traced here: 665 us
  waiting for transfers between devices  545 us (82%)
  local copies, waits for them, and re-layouts  43.1 us (6%)
  starting transfers between devices  28.2 us (4%)
  matrix products  21.2 us (3%)
  between operations  16.7 us (3%)
  other arithmetic  9.3 us (1%)
    all_to_all x1, waiting for transfers between devices, screen_guide(): lax.all_to_all(jnp.stack(lax.axis_size(dev_axis) * [view], axis=0), dev_a...  326 us
    unnamed x2, waiting for transfers between devices  218 us
    unnamed x17, local copies, waits for them, and re-layouts  35.1 us
    ppermute x2, starting transfers between devices, from_partner(): lax.ppermute(shard, axis, [(i, i ^ 1 << apart) for i in range(lax.axis_si...  17.8 us
  transfers between devices with their start and end apart: 4, of which 3 were waited for; matrix products, arithmetic and copies ran while one was open for 2% of the time, Pallas kernels for 0%

profile of v1, /device:TPU:32, one launch (start us, length us, event | category | flops | bytes accessed | tf_op | source)
XLA Modules:
  0.0 665.1 jit_solution(12232773841988195577)
XLA Ops:
  7.2 0.0 copy-start
  8.0 1.5 fusion.16
  9.5 6.0 stack.5
  15.5 10.3 %all-to-all-start = ((bf16[16,160,2560]{2,1,0:T(8,128)(2,1)}), bf16[16,160,2560]{2,1,0:T(8,128)(2,1)}, u32[]{:S(2)}, u32[]{:S(2)}) async-start(bf16[16,160,2560]{2,1,0:T(8,128)(2,1)} %stack.5), calls=%async_computation | async-start | bytes 26214400 | tf_op jit(solution)/shard_map/all_to_all | solution.py:13
  25.9 0.0 reduce-scatter.4.cloned.1.call-start
  25.9 4.0 copy.19
  29.9 4.1 copy.20
  34.0 325.6 %all-to-all-done = bf16[16,160,2560]{2,1,0:T(8,128)(2,1)} async-done(((bf16[16,160,2560]{2,1,0:T(8,128)(2,1)}), bf16[16,160,2560]{2,1,0:T(8,128)(2,1)}, u32[]{:S(2)}, u32[]{:S(2)}) %all-to-all-start) | async-done | bytes 13107232 | tf_op jit(solution)/shard_map/all_to_all | solution.py:13
  359.6 0.0 copy-done
  359.6 10.8 %multiply_reduce_fusion = (f32[384]{0:T(512)S(1)}, f32[384,2560]{0,1:T(8,128)S(1)}) fusion(bf16[2560,2560]{1,0:T(8,128)(2,1)} %bitcast.4, bf16[1,384,2560]{2,1,0:T(8,128)(2,1)S(1)} %copy-done, bf16[1,384,2560]{1,2,0:T(8,128)(2,1)} %copy.19), kind=kOutput, calls=%fused_computation.10 | convolution fusion | flops 5037096448 | bytes 20973056 | tf_op jit(solution)/shard_map/dot_general | solution.py:37
  370.4 0.0 copy-done.2
  370.4 0.0 copy-done.4
  370.4 0.7 fusion.4
  371.1 10.4 %fusion = bf16[2560,2560]{0,1:T(8,128)(2,1)} fusion(f32[384,2560]{0,1:T(8,128)S(1)} %get-tuple-element.68, bf16[1,384,2560]{1,2,0:T(8,128)(2,1)S(1)} %copy-done.2, bf16[1,384,2560]{2,1,0:T(8,128)(2,1)S(1)} %copy-done, f32[384]{0:T(512)S(1)} %broadcast_multiply_fusion, f32[2560]{0:T(1024)S(1)} %copy-done.4, f32[384]{0:T(512)S(1)} %add_rsqrt_fusion), kind=kOutput, calls=%fused_computation.1 | convolution fusion | flops 5046599680 | bytes 20984832 | tf_op jit(solution)/shard_map/dot_general | solution.py:48
  381.6 17.6 %copy.27 = bf16[2560,2560]{1,0:T(8,128)(2,1)} copy(bf16[2560,2560]{0,1:T(8,128)(2,1)} %fusion) | data formatting | bytes 26214400
  399.2 0.0 reduce-scatter.4.cloned.1.call-update
  399.2 1.4 copy-done.3
  400.6 2.0 copy.18
  403.3 218.4 %reduce-scatter.4.cloned.1.call-done = bf16[160,2560]{1,0:T(8,128)(2,1)} async-done(((bf16[2560,2560]{1,0:T(8,128)(2,1)}), bf16[160,2560]{1,0:T(8,128)(2,1)}) %reduce-scatter.4.cloned.1.call-update) | async-done | bytes 819216
  621.7 1.5 copy.28
  623.2 3.5 bitcast_subtract_fusion
  626.7 22.4 %conditional.4 = (bf16[160,2560]{1,0:T(8,128)(2,1)}, f32[1]{0:T(128)}) conditional(s32[]{:T(128)} %bitcast.9, (f32[160,2560]{0,1:T(8,128)}, f32[1]{0:T(128)}) %tuple.50, (f32[160,2560]{0,1:T(8,128)}, f32[1]{0:T(128)}) %tuple.50, (f32[160,2560]{0,1:T(8,128)}, f32[1]{0:T(128)}) %tuple.50, (f32[160,2560]{0,1:T(8,128)}, ...), branch_computations={%region_3.0_spmd, %region_4.0_spmd, %region_5.0_spmd, %region_6.0_... | conditional | flops 2 | bytes 5734516
  626.7 1.9 copy.21
  628.6 1.6 collective-permute-start
  630.8 16.2 %collective-permute-start.1 = (bf16[1]{0:T(256)(128)(2,1)}, bf16[1]{0:T(256)(128)(2,1)}, u32[]{:S(2)}, u32[]{:S(2)}) collective-permute-start(bf16[1]{0:T(256)(128)(2,1)} %convert_element_type.73), channel_id=1, source_target_pairs={{0,16},{16,0},{32,48},{48,32},{64,80},{80,64},{96,112},{112,96},{1... | collective-permute-start | bytes 14 | tf_op jit(solution)/shard_map/cond/branch_0_fun/ppermute | solution.py:30
  647.1 1.0 collective-permute-done.1
  648.8 0.0 collective-permute-done
  649.0 1.5 copy.25
  650.6 0.0 copy-start.1
  650.6 3.6 fusion.8
  654.2 3.0 copy.26
  657.1 0.0 copy-done.1
  (5 shorter events, 0.0 us)
Async XLA Ops:
  7.2 352.4 %copy-start = (bf16[1,384,2560]{2,1,0:T(8,128)(2,1)S(1)}, bf16[1,384,2560]{2,1,0:T(8,128)(2,1)}, u32[]{:S(2)}) copy-start(bf16[1,384,2560]{2,1,0:T(8,128)(2,1)} %param.11) | copy-start | bytes 5898244
  15.5 344.1 %all-to-all-start = ((bf16[16,160,2560]{2,1,0:T(8,128)(2,1)}), bf16[16,160,2560]{2,1,0:T(8,128)(2,1)}, u32[]{:S(2)}, u32[]{:S(2)}) async-start(bf16[16,160,2560]{2,1,0:T(8,128)(2,1)} %stack.5), calls=%async_computation | async-start | bytes 26214400 | tf_op jit(solution)/shard_map/all_to_all | solution.py:13
  25.9 595.8 %reduce-scatter.4.cloned.1.call-start = ((), (), s32[]{:S(2)}) async-start(), calls=%async_computation.2 | async-start | bytes 13926400
  359.6 10.8 %copy-start.2 = (bf16[1,384,2560]{1,2,0:T(8,128)(2,1)S(1)}, bf16[1,384,2560]{1,2,0:T(8,128)(2,1)}, u32[]{:S(2)}) copy-start(bf16[1,384,2560]{1,2,0:T(8,128)(2,1)} %copy.20) | copy-start | bytes 5898244
  359.6 10.8 %copy-start.4 = (f32[2560]{0:T(1024)S(1)}, f32[2560]{0:T(1024)}, u32[]{:S(2)}) copy-start(f32[2560]{0:T(1024)} %param.14) | copy-start | bytes 30724
  399.2 1.4 copy-start.3
  628.6 20.2 %collective-permute-start = (bf16[160,2560]{1,0:T(8,128)(2,1)S(1)}, bf16[160,2560]{1,0:T(8,128)(2,1)}, u32[]{:S(2)}, u32[]{:S(2)}) collective-permute-start(bf16[160,2560]{1,0:T(8,128)(2,1)S(1)} %copy.21), channel_id=1, source_target_pairs={{0,16},{16,0},{32,48},{48,32},{64,80},{80,64},{96,112},{112,96},{1... | collective-permute-start | bytes 2457608 | tf_op jit(solution)/shard_map/cond/branch_0_fun/ppermute | solution.py:30
  630.8 17.3 %collective-permute-start.1 = (bf16[1]{0:T(256)(128)(2,1)}, bf16[1]{0:T(256)(128)(2,1)}, u32[]{:S(2)}, u32[]{:S(2)}) collective-permute-start(bf16[1]{0:T(256)(128)(2,1)} %convert_element_type.73), channel_id=1, source_target_pairs={{0,16},{16,0},{32,48},{48,32},{64,80},{80,64},{96,112},{112,96},{1... | collective-permute-start | bytes 14 | tf_op jit(solution)/shard_map/cond/branch_0_fun/ppermute | solution.py:30
  650.6 6.6 copy-start.1
Sparse Core Ops, SparseCore 0:
  399.3 222.3 reduce-scatter.3
